TPU v7x, 512 devices: a whole 4x4x16 slice. The times are simulated.
512 devices in a mesh: dp: 16 (over z), owner: 32 (over x, y, core).
Axes of the slice: x: 4, y: 4, z: 16, core: 2. Of those that a mesh axis runs over, the one named last changes fastest.
Arguments:
- tokens: bfloat16 [65536, 8192], P(('dp', 'owner')), may hold values from -6 to 6
- residual: bfloat16 [65536, 8192], P(('dp', 'owner')), may hold values from -6 to 6
- token_adapter_index: int32 [65536, 1], P(('dp', 'owner')), may hold values from 0 to 31; in each aligned block of 128 rows (0 to 127, 128 to 255, ...) at most 6 rows name the same one
- adapter_down_weight: bfloat16 [32, 64, 8192], P('owner', None, 'dp'), may hold values from -0.0625 to 0.0625
- adapter_up_weight: bfloat16 [32, 64, 8192], P('owner', None, 'dp'), may hold values from -0.75 to 0.75
- down_moment_first: bfloat16 [32, 64, 8192], P('owner', None, 'dp'), may hold values from -270 to 270
- down_moment_second: bfloat16 [32, 64, 8192], P('owner', None, 'dp'), may hold values from 816 to 24576
- up_moment_first: bfloat16 [32, 64, 8192], P('owner', None, 'dp'), may hold values from -27.125 to 27.125
- up_moment_second: bfloat16 [32, 64, 8192], P('owner', None, 'dp'), may hold values from 6.125 to 204
Outputs:
- down_update: float32 [32, 64, 8192], P('owner', None, 'dp')
- up_update: float32 [32, 64, 8192], P('owner', None, 'dp')
- token_loss: float32 [65536], P(('dp', 'owner'))
Inputs may be any that keep to these rules, and one draw needn't show every extreme that they name: `token_adapter_index`: of the 128 rows of one device, at most 6 name one adapter, and in some devices one adapter is named by exactly 6.
All inputs are finite; a program needn't handle non-finite values.
Results may differ from a plain program's by a relative error of at most 0.0091.
Values may be sent and summed in bfloat16 or wider, within the bound.
No kernel may reach another device: no remote copies, remote signals or barrier semaphores. Data moves between devices by JAX's collectives and lax.ppermute only.
A program may use at most 128 MiB of HBM per device.

v0:
```python
import jax
import jax.numpy as jnp
from jax import lax
from jax.sharding import PartitionSpec as P

adapter_scale = 0.5
adam_eps = 1e-08


def adam_update(grad, first, second):
    first_new = 0.9 * first.astype(jnp.float32) + 0.1 * grad
    second_new = 0.95 * second.astype(jnp.float32) + 0.05 * grad * grad
    return first_new / (jnp.sqrt(second_new) + adam_eps)


def body(
    tokens,
    residual,
    token_adapter_index,
    adapter_down_weight,
    adapter_up_weight,
    down_moment_first,
    down_moment_second,
    up_moment_first,
    up_moment_second,
):
    owner_index = lax.axis_size("owner")
    tok_rows = tokens.shape[0]
    model_width_value = tokens.shape[1]
    column_span = adapter_down_weight.shape[2]
    slot_capacity = max(2, 3 * tok_rows // (2 * owner_index))
    route_ids = token_adapter_index[:, 0]
    member = (route_ids[:, None] == jnp.arange(owner_index, dtype=jnp.int32)[None, :]).astype(
        jnp.int32
    )
    before = jnp.cumsum(member, axis=0) - member
    within = jnp.sum(before * member, axis=1)
    target = route_ids * slot_capacity + within
    dispatch = (
        jnp.arange(owner_index * slot_capacity, dtype=jnp.int32)[:, None] == target[None, :]
    ).astype(jnp.bfloat16)

    def placed_rows(row_block):
        return jnp.dot(dispatch, row_block, preferred_element_type=jnp.float32).astype(jnp.bfloat16)

    down_full, up_weight_whole = (
        lax.all_gather(adapter_down_weight, "dp", axis=2, tiled=True),
        lax.all_gather(adapter_up_weight, "dp", axis=2, tiled=True),
    )
    down_full = down_full[0]
    up_weight_whole = up_weight_whole[0]

    def spread(row_block):
        return placed_rows(row_block).reshape(owner_index, slot_capacity, model_width_value)

    arrived = lax.all_to_all(
        spread(tokens), "owner", split_axis=0, concat_axis=0, tiled=True
    ).reshape(owner_index * slot_capacity, model_width_value)
    hidden_state = lax.dot_general(
        arrived, down_full, (((1,), (1,)), ((), ())), preferred_element_type=jnp.float32
    ).astype(jnp.bfloat16)
    adapter_output = (
        adapter_scale * jnp.dot(hidden_state, up_weight_whole, preferred_element_type=jnp.float32)
    ).astype(jnp.bfloat16)
    hidden_state, adapter_output = (hidden_state, adapter_output)
    returned = lax.all_to_all(
        adapter_output.reshape(owner_index, slot_capacity, model_width_value),
        "owner",
        split_axis=0,
        concat_axis=0,
        tiled=True,
    )
    returned = returned.reshape(owner_index * slot_capacity, model_width_value)
    adapter_home_index = lax.dot_general(
        dispatch, returned, (((0,), (0,)), ((), ())), preferred_element_type=jnp.float32
    )
    shifted_index = residual.astype(jnp.float32) + adapter_home_index
    token_loss = jnp.mean(0.5 * shifted_index * shifted_index, axis=1)
    output_gradient = lax.all_to_all(
        spread(shifted_index.astype(jnp.bfloat16)), "owner", split_axis=0, concat_axis=0, tiled=True
    )
    output_gradient = output_gradient.reshape(owner_index * slot_capacity, model_width_value)
    up_gradient = adapter_scale * lax.dot_general(
        hidden_state, output_gradient, (((0,), (0,)), ((), ())), preferred_element_type=jnp.float32
    )
    hidden_gradient = (
        adapter_scale
        * lax.dot_general(
            output_gradient,
            up_weight_whole,
            (((1,), (1,)), ((), ())),
            preferred_element_type=jnp.float32,
        )
    ).astype(jnp.bfloat16)
    down_grad = lax.dot_general(
        hidden_gradient, arrived, (((0,), (0,)), ((), ())), preferred_element_type=jnp.float32
    )
    summed_down, summed_up = lax.psum((down_grad, up_gradient), "dp")
    offset = lax.axis_index("dp") * column_span
    down_share = lax.dynamic_slice_in_dim(summed_down, offset, column_span, 1)
    up_share = lax.dynamic_slice_in_dim(summed_up, offset, column_span, 1)
    down_update = adam_update(down_share, down_moment_first[0], down_moment_second[0])
    up_update = adam_update(up_share, up_moment_first[0], up_moment_second[0])
    return (down_update[None], up_update[None], token_loss)


def solution(mesh):
    return jax.shard_map(
        body,
        mesh=mesh,
        in_specs=(
            P(("dp", "owner"), None),
            P(("dp", "owner"), None),
            P(("dp", "owner"), None),
            P("owner", None, "dp"),
            P("owner", None, "dp"),
            P("owner", None, "dp"),
            P("owner", None, "dp"),
            P("owner", None, "dp"),
            P("owner", None, "dp"),
        ),
        out_specs=(P("owner", None, "dp"), P("owner", None, "dp"), P(("dp", "owner"))),
        check_vma=False,
    )
```

profile of v0, /device:TPU:6, one launch (start us, length us, event | category | flops | bytes accessed | tf_op | source)
XLA Modules:
  0.0 467.8 jit_solution(18413843679098739913)
XLA Ops:
  7.9 0.7 fusion.19
  8.8 0.8 select_reduce_fusion
  10.3 2.6 convolution_convert_fusion.1
  12.9 4.9 %reshape.44 = bf16[32,6,8192]{2,1,0:T(8,128)(2,1)} reshape(bf16[192,8192]{1,0:T(8,128)(2,1)} %convolution_convert_fusion.1) | data formatting | bytes 6291456 | tf_op jit(solution)/shard_map/reshape | solution.py:54
  17.8 10.4 %all-to-all-start = ((bf16[32,6,8192]{2,1,0:T(8,128)(2,1)}), bf16[32,6,8192]{2,1,0:T(8,128)(2,1)}, u32[]{:S(2)}, u32[]{:S(2)}) async-start(bf16[32,6,8192]{2,1,0:T(8,128)(2,1)} %reshape.44), calls=%async_computation | async-start | bytes 8388608 | tf_op jit(solution)/shard_map/all_to_all | solution.py:56
  28.3 0.7 all-gather.5.cloned.1.call-update
  29.1 50.0 %all-to-all-done = bf16[32,6,8192]{2,1,0:T(8,128)(2,1)} async-done(((bf16[32,6,8192]{2,1,0:T(8,128)(2,1)}), bf16[32,6,8192]{2,1,0:T(8,128)(2,1)}, u32[]{:S(2)}, u32[]{:S(2)}) %all-to-all-start) | async-done | bytes 3145760 | tf_op jit(solution)/shard_map/all_to_all | solution.py:56
  79.1 4.9 %reshape.45 = bf16[192,8192]{1,0:T(8,128)(2,1)} reshape(bf16[32,6,8192]{2,1,0:T(8,128)(2,1)} %all-to-all-done) | data formatting | bytes 6291456 | tf_op jit(solution)/shard_map/reshape | solution.py:58
  84.0 1.3 all-gather.3.cloned.1.call-done
  85.3 3.3 convolution_convert_fusion.2
  88.6 66.5 %all-gather.5.cloned.1.call-done = bf16[1,64,8192]{2,1,0:T(8,128)(2,1)} async-done(((bf16[1,64,512]{2,1,0:T(8,128)(2,1)}), bf16[1,64,8192]{2,1,0:T(8,128)(2,1)}) %all-gather.5.cloned.1.call-update) | async-done | bytes 1048592 | tf_op jit(solution)/shard_map/all_gather | solution.py:48
  155.0 3.9 fusion
  158.9 4.9 %reshape.46 = bf16[32,6,8192]{2,1,0:T(8,128)(2,1)} reshape(bf16[192,8192]{1,0:T(8,128)(2,1)} %fusion) | data formatting | bytes 6291456 | tf_op jit(solution)/shard_map/reshape | solution.py:67
  163.8 56.6 %all_to_all.15 = bf16[32,6,8192]{2,1,0:T(8,128)(2,1)} all-to-all(bf16[32,6,8192]{2,1,0:T(8,128)(2,1)} %reshape.46), channel_id=1, replica_groups=mesh['dp'=16,'owner'=32] {'owner'}, dimensions={0} | all-to-all | bytes 6291456 | tf_op jit(solution)/shard_map/all_to_all | solution.py:66
  220.4 4.9 %reshape.47 = bf16[192,8192]{1,0:T(8,128)(2,1)} reshape(bf16[32,6,8192]{2,1,0:T(8,128)(2,1)} %all_to_all.15) | data formatting | bytes 6291456 | tf_op jit(solution)/shard_map/reshape | solution.py:73
  225.2 3.9 fusion.1
  229.1 2.6 convolution_convert_fusion
  231.7 4.9 %reshape.48 = bf16[32,6,8192]{2,1,0:T(8,128)(2,1)} reshape(bf16[192,8192]{1,0:T(8,128)(2,1)} %convolution_convert_fusion) | data formatting | bytes 6291456 | tf_op jit(solution)/shard_map/reshape | solution.py:54
  236.6 55.2 %all_to_all.16 = bf16[32,6,8192]{2,1,0:T(8,128)(2,1)} all-to-all(bf16[32,6,8192]{2,1,0:T(8,128)(2,1)} %reshape.48), channel_id=1, replica_groups=mesh['dp'=16,'owner'=32] {'owner'}, dimensions={0} | all-to-all | bytes 6291456 | tf_op jit(solution)/shard_map/all_to_all | solution.py:79
  291.8 4.9 %reshape.49 = bf16[192,8192]{1,0:T(8,128)(2,1)} reshape(bf16[32,6,8192]{2,1,0:T(8,128)(2,1)} %all_to_all.16) | data formatting | bytes 6291456 | tf_op jit(solution)/shard_map/reshape | solution.py:82
  296.7 4.0 convolution_multiply_fusion.1
  300.7 6.5 %fusion.4 = f32[64,8192]{1,0:T(8,128)} fusion(bf16[192,8192]{1,0:T(8,128)(2,1)} %reshape.45, bf16[192,8192]{1,0:T(8,128)(2,1)} %reshape.49, bf16[1,64,8192]{2,1,0:T(8,128)(2,1)S(1)} %copy-done.1), kind=kOutput, calls=%fused_computation.12 | convolution fusion | flops 402677760 | bytes 9437184 | tf_op jit(solution)/shard_map/dot_general | solution.py:95
  307.8 151.6 %all-reduce.3.cloned.1.call-done = (f32[64,8192]{1,0:T(8,128)}, f32[64,8192]{1,0:T(8,128)}) async-done(((f32[64,8192]{1,0:T(8,128)}, f32[64,8192]{1,0:T(8,128)}), (f32[64,8192]{1,0:T(8,128)}, f32[64,8192]{1,0:T(8,128)})) %all-reduce.3.cloned.1.call-update) | async-done | bytes 4194320 | tf_op jit(solution)/shard_map/psum | solution.py:98
  459.4 1.8 fusion.13
  (20 shorter events, 2.2 us)
Async XLA Ops:
  7.2 3.2 copy-start
  7.2 78.1 %all-gather.3.cloned.1.call-start = ((), (), s32[]{:S(2)}) async-start(), calls=%async_computation.3 | async-start | bytes 1114112 | tf_op jit(solution)/shard_map/all_gather | solution.py:47
  17.8 61.2 %all-to-all-start = ((bf16[32,6,8192]{2,1,0:T(8,128)(2,1)}), bf16[32,6,8192]{2,1,0:T(8,128)(2,1)}, u32[]{:S(2)}, u32[]{:S(2)}) async-start(bf16[32,6,8192]{2,1,0:T(8,128)(2,1)} %reshape.44), calls=%async_computation | async-start | bytes 8388608 | tf_op jit(solution)/shard_map/all_to_all | solution.py:56
  28.3 126.8 %all-gather.5.cloned.1.call-start = ((), (), s32[]{:S(2)}) async-start(), calls=%async_computation.4 | async-start | bytes 1114112 | tf_op jit(solution)/shard_map/all_gather | solution.py:48
  29.0 430.4 %all-reduce.3.cloned.1.call-start = ((), (), s32[]{:S(2)}) async-start(), calls=%async_computation.5 | async-start | bytes 8388608 | tf_op jit(solution)/shard_map/psum | solution.py:98
  296.7 4.0 copy-start.1
  307.2 152.2 %copy-start.2 = (bf16[1,64,512]{2,1,0:T(8,128)(2,1)S(1)}, bf16[1,64,512]{2,1,0:T(8,128)(2,1)}, u32[]{:S(2)}) copy-start(bf16[1,64,512]{2,1,0:T(8,128)(2,1)} %param.15) | copy-start | bytes 196612
  307.2 152.2 %copy-start.3 = (bf16[1,64,512]{2,1,0:T(8,128)(2,1)S(1)}, bf16[1,64,512]{2,1,0:T(8,128)(2,1)}, u32[]{:S(2)}) copy-start(bf16[1,64,512]{2,1,0:T(8,128)(2,1)} %param.14) | copy-start | bytes 196612
  307.2 152.2 %copy-start.4 = (bf16[1,64,512]{2,1,0:T(8,128)(2,1)S(1)}, bf16[1,64,512]{2,1,0:T(8,128)(2,1)}, u32[]{:S(2)}) copy-start(bf16[1,64,512]{2,1,0:T(8,128)(2,1)} %param.17) | copy-start | bytes 196612
  307.2 152.2 %copy-start.5 = (bf16[1,64,512]{2,1,0:T(8,128)(2,1)S(1)}, bf16[1,64,512]{2,1,0:T(8,128)(2,1)}, u32[]{:S(2)}) copy-start(bf16[1,64,512]{2,1,0:T(8,128)(2,1)} %param.16) | copy-start | bytes 196612
Sparse Core Ops, SparseCore 0:
  10.1 75.1 all-gather.2
  87.4 67.6 all-gather.4
  307.4 151.9 all-reduce.2
where the time goes:
time: 469 us; the launch traced here: 468 us
  waiting for transfers between devices  271 us (58%)
  blocking collectives  112 us (24%)
  local copies, waits for them, and re-layouts  29.4 us (6%)
  matrix products  26.8 us (6%)
  between operations  13.8 us (3%)
  starting transfers between devices  10.5 us (2%)
  other arithmetic  4.76 us (1%)
    psum x1, waiting for transfers between devices, body(): summed_down, summed_up = lax.psum((down_grad, up_gradient), 'dp')  152 us
    all_gather x1, waiting for transfers between devices, body(): lax.all_gather(adapter_up_weight, 'dp', axis=2, tiled=True)  66.5 us
    all_to_all x1, blocking collectives, body(): lax.all_to_all(adapter_output.reshape(owner_index, slot_capacity, model_w...  56.6 us
    all_to_all x1, blocking collectives, body(): lax.all_to_all(spread(shifted_index.astype(jnp.bfloat16)), 'owner', split...  55.2 us
    all_to_all x1, waiting for transfers between devices, body(): lax.all_to_all(spread(tokens), 'owner', split_axis=0, concat_axis=0, tile...  50 us
    all_to_all x1, starting transfers between devices, body(): lax.all_to_all(spread(tokens), 'owner', split_axis=0, concat_axis=0, tile...  10.4 us
    reshape x2, local copies, waits for them, and re-layouts, spread(): placed_rows(row_block)  9.78 us
  transfers between devices with their start and end apart: 4, of which 4 were waited for; matrix products, arithmetic and copies ran while one was open for 4% of the time, Pallas kernels for 0%

commit v1 on v0

--- a/solution.py
+++ b/solution.py
@@ -45,7 +45,9 @@
 
     down_full, up_weight_whole = (
         lax.all_gather(adapter_down_weight, "dp", axis=2, tiled=True),
-        lax.all_gather(adapter_up_weight, "dp", axis=2, tiled=True),
+        jnp.concatenate(
+            lax.all_to_all(jnp.stack([adapter_up_weight] * lax.axis_size("dp")), "dp", 0, 0), axis=2
+        ),
     )
     down_full = down_full[0]
     up_weight_whole = up_weight_whole[0]

time: 469 us -> 493 us (1.051)
  blocking collectives: 112 us -> 170 us
  waiting for transfers between devices: 271 us -> 231 us
    all_gather x1, waiting for transfers between devices: 1.28 us -> 79.4 us  [body(): lax.all_gather(adapter_down_weight, 'dp', axis=2, tiled=True)]
    all_gather x1 -> x0, waiting for transfers between devices: 66.5 us -> none  [body(): lax.all_gather(adapter_up_weight, 'dp', axis=2, tiled=True)]
    all_to_all x0 -> x1, blocking collectives: none -> 59.5 us  [body(): lax.all_to_all(spread(tokens), 'owner', split_axis=0, concat_axis=0, tile...]
    all_to_all x1, waiting for transfers between devices: 50 us -> 0.01 us  [body(): lax.all_to_all(jnp.stack([adapter_up_weight] * lax.axis_size('dp')), 'dp'...]
  transfers between devices with their start and end apart: 4 -> 3, of which waited for: 4 -> 2; matrix products, arithmetic and copies ran while one was open for 4% -> 2% of each run, Pallas kernels for 0% -> 0%
where the time goes in v1:
time: 493 us; the launch traced here: 492 us
  waiting for transfers between devices  231 us (47%)
  blocking collectives  170 us (34%)
  local copies, waits for them, and re-layouts  32.7 us (7%)
  matrix products  25.6 us (5%)
  between operations  14.1 us (3%)
  starting transfers between devices  12.6 us (3%)
    psum x1, waiting for transfers between devices, body(): summed_down, summed_up = lax.psum((down_grad, up_gradient), 'dp')  151 us
    all_gather x1, waiting for transfers between devices, body(): lax.all_gather(adapter_down_weight, 'dp', axis=2, tiled=True)  79.4 us
    all_to_all x1, blocking collectives, body(): lax.all_to_all(spread(tokens), 'owner', split_axis=0, concat_axis=0, tile...  59.5 us
    all_to_all x1, blocking collectives, body(): lax.all_to_all(adapter_output.reshape(owner_index, slot_capacity, model_w...  55.5 us
    all_to_all x1, blocking collectives, body(): lax.all_to_all(spread(shifted_index.astype(jnp.bfloat16)), 'owner', split...  55.2 us
    all_to_all x1, starting transfers between devices, body(): lax.all_to_all(jnp.stack([adapter_up_weight] * lax.axis_size('dp')), 'dp'...  12.5 us
  transfers between devices with their start and end apart: 3, of which 2 were waited for; matrix products, arithmetic and copies ran while one was open for 2% of the time, Pallas kernels for 0%

profile of v1, /device:TPU:6, one launch (start us, length us, event | category | flops | bytes accessed | tf_op | source)
XLA Modules:
  0.0 491.6 jit_solution(5974878436663460717)
XLA Ops:
  7.2 0.9 fusion.16
  9.7 2.6 convolution_convert_fusion.1
  12.4 4.9 reshape.50
  17.2 59.5 %all_to_all.20 = bf16[32,6,8192]{2,1,0:T(8,128)(2,1)} all-to-all(bf16[32,6,8192]{2,1,0:T(8,128)(2,1)} %reshape.50), channel_id=1, replica_groups=mesh['dp'=16,'owner'=32] {'owner'}, dimensions={0} | all-to-all | bytes 6291456 | tf_op jit(solution)/shard_map/all_to_all | solution.py:58
  76.7 1.1 stack.2
  77.8 12.5 %all-to-all-start.1 = ((bf16[16,1,64,512]{3,2,1,0:T(8,128)(2,1)}), bf16[16,1,64,512]{3,2,1,0:T(8,128)(2,1)S(1)}, u32[]{:S(2)}, u32[]{:S(2)}) async-start(bf16[16,1,64,512]{3,2,1,0:T(8,128)(2,1)} %stack.2), calls=%async_computation.1 | async-start | bytes 2097152 | tf_op jit(solution)/shard_map/all_to_all | solution.py:49
  91.2 5.0 %reshape.51 = bf16[192,8192]{1,0:T(8,128)(2,1)} reshape(bf16[32,6,8192]{2,1,0:T(8,128)(2,1)} %all_to_all.20) | data formatting | bytes 6291456 | tf_op jit(solution)/shard_map/reshape | solution.py:60
  96.1 79.4 %all-gather.2.cloned.1.call-done = bf16[1,64,8192]{2,1,0:T(8,128)(2,1)} async-done(((bf16[1,64,512]{2,1,0:T(8,128)(2,1)}), bf16[1,64,8192]{2,1,0:T(8,128)(2,1)}) %all-gather.2.cloned.1.call-update) | async-done | bytes 1048592 | tf_op jit(solution)/shard_map/all_gather | solution.py:47
  175.5 3.3 convolution_convert_fusion.2
  178.8 1.0 copy-done.1
  179.7 1.3 copy.13
  181.1 2.7 fusion
  183.7 4.9 reshape.53
  188.6 55.5 %all_to_all.21 = bf16[32,6,8192]{2,1,0:T(8,128)(2,1)} all-to-all(bf16[32,6,8192]{2,1,0:T(8,128)(2,1)} %reshape.53), channel_id=1, replica_groups=mesh['dp'=16,'owner'=32] {'owner'}, dimensions={0} | all-to-all | bytes 6291456 | tf_op jit(solution)/shard_map/all_to_all | solution.py:68
  244.1 4.9 reshape.54
  249.0 3.9 fusion.1
  252.8 2.6 convolution_convert_fusion
  255.5 4.9 reshape.55
  260.3 55.2 %all_to_all.22 = bf16[32,6,8192]{2,1,0:T(8,128)(2,1)} all-to-all(bf16[32,6,8192]{2,1,0:T(8,128)(2,1)} %reshape.55), channel_id=1, replica_groups=mesh['dp'=16,'owner'=32] {'owner'}, dimensions={0} | all-to-all | bytes 6291456 | tf_op jit(solution)/shard_map/all_to_all | solution.py:81
  315.5 4.9 reshape.56
  320.4 4.0 convolution_multiply_fusion.1
  324.4 6.6 %fusion.4 = f32[64,8192]{1,0:T(8,128)} fusion(bf16[192,8192]{1,0:T(8,128)(2,1)} %reshape.51, bf16[192,8192]{1,0:T(8,128)(2,1)} %reshape.56, bf16[64,8192]{1,0:T(8,128)(2,1)S(1)} %bitcast.40), kind=kOutput, calls=%fused_computation.12 | convolution fusion | flops 402677760 | bytes 9437184 | tf_op jit(solution)/shard_map/dot_general | solution.py:97
  331.5 151.4 %all-reduce.3.cloned.1.call-done = (f32[64,8192]{1,0:T(8,128)}, f32[64,8192]{1,0:T(8,128)}) async-done(((f32[64,8192]{1,0:T(8,128)}, f32[64,8192]{1,0:T(8,128)}), (f32[64,8192]{1,0:T(8,128)}, f32[64,8192]{1,0:T(8,128)})) %all-reduce.3.cloned.1.call-update) | async-done | bytes 4194320 | tf_op jit(solution)/shard_map/psum | solution.py:100
  482.9 1.8 fusion.10
  (22 shorter events, 3.0 us)
Async XLA Ops:
  7.2 2.6 copy-start
  17.2 59.5 %copy-start.2 = (bf16[1,64,512]{2,1,0:T(8,128)(2,1)S(1)}, bf16[1,64,512]{2,1,0:T(8,128)(2,1)}, u32[]{:S(2)}) copy-start(bf16[1,64,512]{2,1,0:T(8,128)(2,1)} %param.13) | copy-start | bytes 196612
  77.8 100.9 %all-to-all-start.1 = ((bf16[16,1,64,512]{3,2,1,0:T(8,128)(2,1)}), bf16[16,1,64,512]{3,2,1,0:T(8,128)(2,1)S(1)}, u32[]{:S(2)}, u32[]{:S(2)}) async-start(bf16[16,1,64,512]{3,2,1,0:T(8,128)(2,1)} %stack.2), calls=%async_computation.1 | async-start | bytes 2097152 | tf_op jit(solution)/shard_map/all_to_all | solution.py:49
  90.4 85.1 %all-gather.2.cloned.1.call-start = ((), (), s32[]{:S(2)}) async-start(), calls=%async_computation.4 | async-start | bytes 1114112 | tf_op jit(solution)/shard_map/all_gather | solution.py:47
  91.1 391.8 %all-reduce.3.cloned.1.call-start = ((), (), s32[]{:S(2)}) async-start(), calls=%async_computation.5 | async-start | bytes 8388608 | tf_op jit(solution)/shard_map/psum | solution.py:100
  178.8 1.0 copy-start.1
  330.9 152.0 %copy-start.3 = (bf16[1,64,512]{2,1,0:T(8,128)(2,1)S(1)}, bf16[1,64,512]{2,1,0:T(8,128)(2,1)}, u32[]{:S(2)}) copy-start(bf16[1,64,512]{2,1,0:T(8,128)(2,1)} %param.15) | copy-start | bytes 196612
  330.9 152.0 %copy-start.4 = (bf16[1,64,512]{2,1,0:T(8,128)(2,1)S(1)}, bf16[1,64,512]{2,1,0:T(8,128)(2,1)}, u32[]{:S(2)}) copy-start(bf16[1,64,512]{2,1,0:T(8,128)(2,1)} %param.14) | copy-start | bytes 196612
  330.9 152.0 %copy-start.5 = (bf16[1,64,512]{2,1,0:T(8,128)(2,1)S(1)}, bf16[1,64,512]{2,1,0:T(8,128)(2,1)}, u32[]{:S(2)}) copy-start(bf16[1,64,512]{2,1,0:T(8,128)(2,1)} %param.17) | copy-start | bytes 196612
  330.9 152.0 %copy-start.6 = (bf16[1,64,512]{2,1,0:T(8,128)(2,1)S(1)}, bf16[1,64,512]{2,1,0:T(8,128)(2,1)}, u32[]{:S(2)}) copy-start(bf16[1,64,512]{2,1,0:T(8,128)(2,1)} %param.16) | copy-start | bytes 196612
Sparse Core Ops, SparseCore 0:
  93.3 82.1 all-gather.1
  331.1 151.7 all-reduce.2
